TPU v7x, 32 devices: a whole 2x2x4 slice. The times are simulated.
32 devices in a mesh: dom: 8 (over y, x, core), sub: 4 (over z).
Axes of the slice: x: 2, y: 2, z: 4, core: 2. Of those that a mesh axis runs over, the one named last changes fastest.
Arguments:
- vectors: bfloat16 [8192, 1024], P(('dom', 'sub')), may hold values from -8 to 8
- assign: int32 [8192], P(('dom', 'sub')), may hold values from 0 to 32767, as said below
- codes: int32 [8192, 256], P(('dom', 'sub')), may hold values from 0 to 15
- centroids: float32 [32768, 1024], P('dom', 'sub'), may hold values from -4 to 4
- perp_ratio: float32 [32768], P('dom'), may hold values from 0.25 to 0.9
- codebook: float32 [256, 16, 4], P('sub'), may hold values from -4 to 4
- codeword_weight_total: float32 [256, 16], P('sub'), may hold values from 64 to 512
Outputs:
- new_centroids: float32 [32768, 1024], P('dom', 'sub')
- residual: bfloat16 [8192, 1024], P(('dom', 'sub'))
- new_codebook: float32 [256, 16, 4], P('sub')
Inputs may be any that keep to these rules, and one draw needn't show every extreme that they name: `assign`: owner o holds partitions o * 4096 to (o + 1) * 4096 - 1 and o runs over 8 owners. The rows of one device are grouped by owner in increasing owner order; at most 64 rows of one device belong to one owner, and on every device some owner receives exactly 64.
All inputs are finite; a program needn't handle non-finite values.
Results may differ from a plain program's by a relative error of at most 0.001.
Values may be sent and summed in bfloat16 or wider, within the bound.
No kernel may reach another device: no remote copies, remote signals or barrier semaphores. Data moves between devices by JAX's collectives and lax.ppermute only.
A program may use at most 128 MiB of HBM per device.

v0:
```python
import jax
import jax.numpy as jnp
from jax import lax
from jax.sharding import PartitionSpec as P

K = 16
DS = 4
ITERS = 4


def per_device(vectors, assign, codes, centroids, perp_ratio, codebook, codeword_weight_total):
    owners = lax.axis_size("dom")
    sub_count = lax.axis_size("sub")
    rows_dev, row_width = vectors.shape
    part_local = centroids.shape[0]
    columns = centroids.shape[1]
    capacity = 2 * rows_dev // owners
    owner_of = assign // part_local
    owner_mask = owner_of[:, None] == jnp.arange(owners, dtype=jnp.int32)[None, :]
    counts = jnp.sum(owner_mask.astype(jnp.int32), axis=0)
    starts = jnp.cumsum(counts) - counts
    first_row_index = jnp.sum(jnp.where(owner_mask, starts[None, :], 0), axis=1)
    position = jnp.arange(rows_dev, dtype=jnp.int32) - first_row_index
    slot_index = owner_of * capacity + position
    source_rows = starts[:, None] + jnp.arange(capacity, dtype=jnp.int32)[None, :]
    usable_slot = jnp.arange(capacity, dtype=jnp.int32)[None, :] < counts[:, None]
    clipped = jnp.minimum(source_rows, rows_dev - 1)
    send_rows = jnp.where(
        usable_slot[:, :, None], jnp.take(vectors, clipped, axis=0), jnp.zeros((), jnp.bfloat16)
    )
    owner_base = (jnp.arange(owners, dtype=jnp.int32) * part_local)[:, None]
    send_ids = jnp.where(usable_slot, jnp.take(assign, clipped, axis=0) - owner_base, part_local)
    split_rows = send_rows.reshape(owners, capacity, sub_count, columns).transpose(0, 2, 1, 3)
    split_rows = split_rows.reshape(owners * sub_count, capacity, columns)
    id_copies = jnp.broadcast_to(send_ids[:, None, :], (owners, sub_count, capacity)).reshape(
        owners * sub_count, capacity
    )
    arrived, arrived_ids = (
        lax.all_to_all(split_rows, ("dom", "sub"), split_axis=0, concat_axis=0, tiled=True),
        lax.all_to_all(id_copies, ("dom", "sub"), split_axis=0, concat_axis=0, tiled=True),
    )
    arrived = arrived.reshape(-1, columns)
    slot_ids = arrived_ids.reshape(-1)
    usable = slot_ids < part_local
    safe_ids = jnp.minimum(slot_ids, part_local - 1)
    as_float = arrived.astype(jnp.float32)
    arrived_count = arrived.shape[0]
    block = 512
    block_count = arrived_count // block
    id_blocks = slot_ids.reshape(block_count, block)
    row_blocks = arrived.reshape(block_count, block, columns)
    part_range = jnp.arange(part_local, dtype=jnp.int32)
    contract_rows = (((0,), (0,)), ((), ()))

    def member_table(ids):
        return (ids[:, None] == part_range[None, :]).astype(jnp.bfloat16)

    def tally_step(carry, inputs):
        ids, rows_b = inputs
        table = member_table(ids)
        count_acc, sum_acc = carry
        count_acc = count_acc + jnp.sum(table, axis=0, dtype=jnp.float32)
        sum_acc = sum_acc + lax.dot_general(
            table, rows_b, contract_rows, preferred_element_type=jnp.float32
        )
        return ((count_acc, sum_acc), None)

    start_tally = (
        jnp.zeros((part_local,), jnp.float32),
        jnp.zeros((part_local, columns), jnp.float32),
    )
    (filled, sum_x), unused = lax.scan(tally_step, start_tally, (id_blocks, row_blocks))

    def project_step(acc, inputs):
        ids, rows_b, weight_b = inputs
        table = member_table(ids).astype(jnp.float32)
        scaled = rows_b.astype(jnp.float32) * weight_b[:, None]
        term = lax.dot_general(
            table,
            scaled,
            contract_rows,
            precision=lax.Precision.HIGHEST,
            preferred_element_type=jnp.float32,
        )
        return (acc + term, None)

    norms = lax.psum(jnp.sum(as_float * as_float, axis=1), "sub")
    floors = jnp.maximum(filled, 1.0)[:, None]
    weight_fractions = perp_ratio[:, None]
    current = centroids
    for iteration in range(ITERS):
        picked = jnp.take(current, safe_ids, axis=0)
        inner_full = lax.psum(jnp.sum(as_float * picked, axis=1), "sub")
        weight = inner_full / (norms + 1e-06)
        weight_blocks = weight.reshape(block_count, block)
        projected, unused = lax.scan(
            project_step,
            jnp.zeros((part_local, columns), jnp.float32),
            (id_blocks, row_blocks, weight_blocks),
        )
        current = (
            current
            - (
                weight_fractions * filled[:, None] * current
                + (1.0 - weight_fractions) * projected
                - sum_x
            )
            / floors
        )
    picked = jnp.take(current, safe_ids, axis=0)
    residual = jnp.where(usable[:, None], as_float - picked, 0.0).astype(jnp.bfloat16)
    residual = residual.reshape(owners, sub_count * capacity, columns)
    outgoing = residual.reshape(owners * sub_count, capacity, columns)
    returned = lax.all_to_all(outgoing, ("dom", "sub"), split_axis=0, concat_axis=0, tiled=True)
    returned = returned.reshape(owners, sub_count, capacity, columns).transpose(0, 2, 1, 3)
    flat_rows = returned.reshape(owners * capacity, row_width)
    residual_rows = jnp.take(flat_rows, slot_index, axis=0)
    m_all = codes.shape[1]
    code_range = jnp.arange(K, dtype=jnp.int32)
    code_member = (codes[:, :, None] == code_range[None, None, :]).astype(jnp.bfloat16)
    pieces = residual_rows.reshape(rows_dev, m_all, DS)
    book_sums = jnp.einsum(
        "rmk,rmd->mkd", code_member, pieces, preferred_element_type=jnp.float32
    ).reshape(m_all * K, DS)
    book_counts = jnp.sum(code_member, axis=0, dtype=jnp.float32).reshape(m_all * K)
    local_sub = codebook.shape[0]
    all_sums, all_counts = lax.psum((book_sums, book_counts), ("dom", "sub"))
    offset = lax.axis_index("sub") * (local_sub * K)
    totals = lax.dynamic_slice_in_dim(all_sums, offset, local_sub * K, 0)
    tallies = lax.dynamic_slice_in_dim(all_counts, offset, local_sub * K, 0)
    weights = codeword_weight_total.reshape(local_sub * K, 1)
    updated = (codebook.reshape(local_sub * K, DS) * weights + totals) / (
        weights + tallies[:, None]
    )
    return (current, residual_rows, updated.reshape(local_sub, K, DS))


def solution(mesh):
    placed = (
        P(("dom", "sub"), None),
        P(("dom", "sub")),
        P(("dom", "sub"), None),
        P("dom", "sub"),
        P("dom"),
        P("sub", None, None),
        P("sub", None),
    )
    return jax.shard_map(
        per_device,
        mesh=mesh,
        in_specs=placed,
        out_specs=(P("dom", "sub"), P(("dom", "sub"), None), P("sub", None, None)),
        check_vma=False,
    )
```

profile of v0, /device:TPU:1, one launch (start us, length us, event | category | flops | bytes accessed | tf_op | source)
XLA Modules:
  0.0 561.8 jit_solution(17518473978738521301)
XLA Ops:
  7.2 0.7 and_select_fusion
  8.4 3.6 gather_fusion
  12.8 7.1 %all-to-all-start = ((s32[32,1,64]{2,1,0:T(1,128)}), s32[32,1,64]{2,1,0:T(1,128)S(1)}, u32[]{:S(2)}, u32[]{:S(2)}) async-start(s32[32,1,64]{2,1,0:T(1,128)} %bitcast.2), calls=%async_computation | async-start | bytes 32768 | tf_op jit(solution)/shard_map/all_to_all | solution.py:40
  20.1 2.1 gather_fusion.1
  22.4 1.0 pad_maximum_fusion
  23.5 3.1 all-to-all-done
  26.5 3.0 all-to-all-start.1
  31.1 10.8 %gather_fusion.3 = f32[2048,256]{1,0:T(8,128)} fusion(f32[4096,256]{1,0:T(8,128)} %param.22, s32[2048]{0:T(1024)S(1)} %fusion.58), kind=kCustom, calls=%fused_computation.clone | custom fusion | bytes 4202496 | tf_op jit(solution)/shard_map/jit(_take)/gather | solution.py:92
  41.9 14.1 %all-to-all-done.1 = bf16[32,64,256]{2,1,0:T(8,128)(2,1)S(1)} async-done(((bf16[32,64,256]{2,1,0:T(8,128)(2,1)}), bf16[32,64,256]{2,1,0:T(8,128)(2,1)S(1)}, u32[]{:S(2)}, u32[]{:S(2)}) %all-to-all-start.1) | async-done | bytes 1048608 | tf_op jit(solution)/shard_map/all_to_all | solution.py:39
  56.4 2.0 fusion.48
  58.4 13.2 %all-reduce = (f32[2048]{0:T(1024)S(1)}, f32[2048]{0:T(1024)S(1)}) all-reduce(f32[2048]{0:T(1024)S(1)} %fusion.48, f32[2048]{0:T(1024)S(1)} %reduce_sum.86), channel_id=1, replica_groups=mesh['dom'=8,'sub'=4] {'sub'}, use_global_device_ids=true, to_apply=%region_6.8 | all-reduce | flops 4096 | bytes 32768 | tf_op jit(solution)/shard_map/psum | solution.py:93
  71.7 39.2 %while.58 = (s32[]{:T(128)}, f32[4096,256]{1,0:T(8,128)}, s32[4,512]{1,0:T(4,128)S(1)}, bf16[4,512,256]{2,1,0:T(8,128)(2,1)S(1)}, f32[4,512]{1,0:T(4,128)S(1)}, /*index=5*/s32[]{:T(128)}, s32[]{:T(128)}) while((s32[]{:T(128)}, f32[4096,256]{1,0:T(8,128)}, s32[4,512]{1,0:T(4,128)S(1)}, bf16[4,512,256]{2,1,0:T(8,128)(2,1)S(1)}, ...), condition=%wide.region_10.12_spmd.clone, body=%wide.region_9.11_spmd.clone.sunk | while | flops 6446907392 | bytes 8663139 | solution.py:96
  71.7 8.6 %fusion.73 = f32[4096,256]{1,0:T(8,128)} fusion(f32[4096,256]{1,0:T(8,128)} %get-tuple-element.532, s32[512]{0:T(512)S(1)} %bitcast.114, pred[]{:T(512)S(6)} %compare.18, f32[512]{0:T(512)S(1)} %bitcast.120, bf16[4,512,256]{2,1,0:T(8,128)(2,1)S(1)} %get-tuple-element.541, s32[]{:T(128)} %get-tuple-element.531), kind=kOutput, calls=%fused_computation.26.clone.1 | convolution fusion | flops 6446907392 | bytes 8654853 | tf_op jit(solution)/shard_map/while/body/eval_jaxpr/dot_general | solution.py:78
  80.3 10.2 %fusion.73 = f32[4096,256]{1,0:T(8,128)} fusion(f32[4096,256]{1,0:T(8,128)} %get-tuple-element.532, s32[512]{0:T(512)S(1)} %bitcast.114, pred[]{:T(512)S(6)} %compare.18, f32[512]{0:T(512)S(1)} %bitcast.120, bf16[4,512,256]{2,1,0:T(8,128)(2,1)S(1)} %get-tuple-element.541, s32[]{:T(128)} %get-tuple-element.531), kind=kOutput, calls=%fused_computation.26.clone.1 | convolution fusion | flops 6446907392 | bytes 8654853 | tf_op jit(solution)/shard_map/while/body/eval_jaxpr/dot_general | solution.py:78
  90.5 10.2 %fusion.73 = f32[4096,256]{1,0:T(8,128)} fusion(f32[4096,256]{1,0:T(8,128)} %get-tuple-element.532, s32[512]{0:T(512)S(1)} %bitcast.114, pred[]{:T(512)S(6)} %compare.18, f32[512]{0:T(512)S(1)} %bitcast.120, bf16[4,512,256]{2,1,0:T(8,128)(2,1)S(1)} %get-tuple-element.541, s32[]{:T(128)} %get-tuple-element.531), kind=kOutput, calls=%fused_computation.26.clone.1 | convolution fusion | flops 6446907392 | bytes 8654853 | tf_op jit(solution)/shard_map/while/body/eval_jaxpr/dot_general | solution.py:78
  100.7 10.2 %fusion.73 = f32[4096,256]{1,0:T(8,128)} fusion(f32[4096,256]{1,0:T(8,128)} %get-tuple-element.532, s32[512]{0:T(512)S(1)} %bitcast.114, pred[]{:T(512)S(6)} %compare.18, f32[512]{0:T(512)S(1)} %bitcast.120, bf16[4,512,256]{2,1,0:T(8,128)(2,1)S(1)} %get-tuple-element.541, s32[]{:T(128)} %get-tuple-element.531), kind=kOutput, calls=%fused_computation.26.clone.1 | convolution fusion | flops 6446907392 | bytes 8654853 | tf_op jit(solution)/shard_map/while/body/eval_jaxpr/dot_general | solution.py:78
  110.8 32.9 %while.57 = (s32[]{:T(128)}, f32[4096]{0:T(1024)S(1)}, f32[4096,256]{1,0:T(8,128)}, s32[4,512]{1,0:T(4,128)S(1)}, bf16[4,512,256]{2,1,0:T(8,128)(2,1)S(1)}, /*index=5*/s32[]{:T(128)}, s32[]{:T(128)}) while((s32[]{:T(128)}, f32[4096]{0:T(1024)S(1)}, f32[4096,256]{1,0:T(8,128)}, s32[4,512]{1,0:T(4,128)S(1)}, ...), condition=%wide.region_4.5_spmd.clone, body=%wide.region_2.4_spmd.clone.sunk | while | flops 1086328832 | bytes 8724576 | solution.py:72
  110.8 4.5 fusion.72
  115.4 2.0 convert_reduce_fusion.4
  117.4 6.7 %fusion.72 = f32[4096,256]{1,0:T(8,128)} fusion(f32[4096,256]{1,0:T(8,128)} %get-tuple-element.512, s32[512]{0:T(512)S(1)} %bitcast.115, pred[]{:T(512)S(6)} %compare.17, bf16[4,512,256]{2,1,0:T(8,128)(2,1)S(1)} %get-tuple-element.521, s32[]{:T(128)} %get-tuple-element.510), kind=kOutput, calls=%fused_computation.17.clone.1 | convolution fusion | flops 1077936128 | bytes 8652805 | tf_op jit(solution)/shard_map/while/body/eval_jaxpr/dot_general | solution.py:63
  124.2 2.0 convert_reduce_fusion.4
  126.2 6.7 %fusion.72 = f32[4096,256]{1,0:T(8,128)} fusion(f32[4096,256]{1,0:T(8,128)} %get-tuple-element.512, s32[512]{0:T(512)S(1)} %bitcast.115, pred[]{:T(512)S(6)} %compare.17, bf16[4,512,256]{2,1,0:T(8,128)(2,1)S(1)} %get-tuple-element.521, s32[]{:T(128)} %get-tuple-element.510), kind=kOutput, calls=%fused_computation.17.clone.1 | convolution fusion | flops 1077936128 | bytes 8652805 | tf_op jit(solution)/shard_map/while/body/eval_jaxpr/dot_general | solution.py:63
  132.9 2.0 convert_reduce_fusion.4
  135.0 6.7 %fusion.72 = f32[4096,256]{1,0:T(8,128)} fusion(f32[4096,256]{1,0:T(8,128)} %get-tuple-element.512, s32[512]{0:T(512)S(1)} %bitcast.115, pred[]{:T(512)S(6)} %compare.17, bf16[4,512,256]{2,1,0:T(8,128)(2,1)S(1)} %get-tuple-element.521, s32[]{:T(128)} %get-tuple-element.510), kind=kOutput, calls=%fused_computation.17.clone.1 | convolution fusion | flops 1077936128 | bytes 8652805 | tf_op jit(solution)/shard_map/while/body/eval_jaxpr/dot_general | solution.py:63
  141.7 2.0 convert_reduce_fusion.4
  143.7 8.6 %divide_subtract_fusion.3 = f32[4096,256]{1,0:T(8,128)} fusion(f32[4096,256]{1,0:T(8,128)} %param.22, f32[4096,256]{1,0:T(8,128)} %get-tuple-element.167, f32[4096,256]{1,0:T(8,128)} %get-tuple-element.166, f32[4096]{0:T(1024)S(1)} %get-tuple-element.344, f32[4096]{0:T(1024)S(1)} %get-tuple-element.345, f32[4096]{0:T(1024)S(1)} %get-tuple-element.343), kind=kLoop, calls=%fused_computation.75 | loop fusion | flops 6291456 | bytes 16826368 | tf_op jit(solution)/shard_map/sub | solution.py:102
  152.3 10.7 %gather_fusion.4 = f32[2048,256]{1,0:T(8,128)} fusion(f32[4096,256]{1,0:T(8,128)} %divide_subtract_fusion.3, s32[2048]{0:T(1024)S(1)} %fusion.58), kind=kCustom, calls=%fused_computation.1.clone | custom fusion | bytes 4202496 | tf_op jit(solution)/shard_map/jit(_take)/gather | solution.py:92
  163.1 2.0 fusion.49
  165.1 7.0 %psum.51 = f32[2048]{0:T(1024)S(1)} all-reduce(f32[2048]{0:T(1024)S(1)} %fusion.49), channel_id=1, replica_groups=mesh['dom'=8,'sub'=4] {'sub'}, use_global_device_ids=true, to_apply=%region_12.14 | all-reduce | flops 2048 | bytes 16384 | tf_op jit(solution)/shard_map/psum | solution.py:93
  172.0 39.2 %while.59 = (s32[]{:T(128)}, f32[4096,256]{1,0:T(8,128)}, s32[4,512]{1,0:T(4,128)S(1)}, bf16[4,512,256]{2,1,0:T(8,128)(2,1)S(1)}, f32[4,512]{1,0:T(4,128)S(1)}, /*index=5*/s32[]{:T(128)}, s32[]{:T(128)}) while((s32[]{:T(128)}, f32[4096,256]{1,0:T(8,128)}, s32[4,512]{1,0:T(4,128)S(1)}, bf16[4,512,256]{2,1,0:T(8,128)(2,1)S(1)}, ...), condition=%wide.region_14.16_spmd.clone, body=%wide.region_13.15_spmd.clone.sunk | while | flops 6446907392 | bytes 8663139 | solution.py:96
  172.1 8.6 %fusion.74 = f32[4096,256]{1,0:T(8,128)} fusion(f32[4096,256]{1,0:T(8,128)} %get-tuple-element.553, s32[512]{0:T(512)S(1)} %bitcast.117, pred[]{:T(512)S(6)} %compare.19, f32[512]{0:T(512)S(1)} %bitcast.121, bf16[4,512,256]{2,1,0:T(8,128)(2,1)S(1)} %get-tuple-element.562, s32[]{:T(128)} %get-tuple-element.552), kind=kOutput, calls=%fused_computation.37.clone.1 | convolution fusion | flops 6446907392 | bytes 8654853 | tf_op jit(solution)/shard_map/while/body/eval_jaxpr/dot_general | solution.py:78
  180.7 10.2 %fusion.74 = f32[4096,256]{1,0:T(8,128)} fusion(f32[4096,256]{1,0:T(8,128)} %get-tuple-element.553, s32[512]{0:T(512)S(1)} %bitcast.117, pred[]{:T(512)S(6)} %compare.19, f32[512]{0:T(512)S(1)} %bitcast.121, bf16[4,512,256]{2,1,0:T(8,128)(2,1)S(1)} %get-tuple-element.562, s32[]{:T(128)} %get-tuple-element.552), kind=kOutput, calls=%fused_computation.37.clone.1 | convolution fusion | flops 6446907392 | bytes 8654853 | tf_op jit(solution)/shard_map/while/body/eval_jaxpr/dot_general | solution.py:78
  190.9 10.2 %fusion.74 = f32[4096,256]{1,0:T(8,128)} fusion(f32[4096,256]{1,0:T(8,128)} %get-tuple-element.553, s32[512]{0:T(512)S(1)} %bitcast.117, pred[]{:T(512)S(6)} %compare.19, f32[512]{0:T(512)S(1)} %bitcast.121, bf16[4,512,256]{2,1,0:T(8,128)(2,1)S(1)} %get-tuple-element.562, s32[]{:T(128)} %get-tuple-element.552), kind=kOutput, calls=%fused_computation.37.clone.1 | convolution fusion | flops 6446907392 | bytes 8654853 | tf_op jit(solution)/shard_map/while/body/eval_jaxpr/dot_general | solution.py:78
  201.0 10.2 %fusion.74 = f32[4096,256]{1,0:T(8,128)} fusion(f32[4096,256]{1,0:T(8,128)} %get-tuple-element.553, s32[512]{0:T(512)S(1)} %bitcast.117, pred[]{:T(512)S(6)} %compare.19, f32[512]{0:T(512)S(1)} %bitcast.121, bf16[4,512,256]{2,1,0:T(8,128)(2,1)S(1)} %get-tuple-element.562, s32[]{:T(128)} %get-tuple-element.552), kind=kOutput, calls=%fused_computation.37.clone.1 | convolution fusion | flops 6446907392 | bytes 8654853 | tf_op jit(solution)/shard_map/while/body/eval_jaxpr/dot_general | solution.py:78
  211.2 8.6 %divide_subtract_fusion.2 = f32[4096,256]{1,0:T(8,128)} fusion(f32[4096,256]{1,0:T(8,128)} %divide_subtract_fusion.3, f32[4096,256]{1,0:T(8,128)} %get-tuple-element.167, f32[4096,256]{1,0:T(8,128)} %get-tuple-element.168, f32[4096]{0:T(1024)S(1)} %get-tuple-element.344, f32[4096]{0:T(1024)S(1)} %get-tuple-element.345, f32[4096]{0:T(1024)S(1)} %get-tuple-element.343), kind=kLoop, calls=%fused_computation.74 | loop fusion | flops 6291456 | bytes 16826368 | tf_op jit(solution)/shard_map/sub | solution.py:102
  219.8 10.7 %gather_fusion.5 = f32[2048,256]{1,0:T(8,128)} fusion(f32[4096,256]{1,0:T(8,128)} %divide_subtract_fusion.2, s32[2048]{0:T(1024)S(1)} %fusion.58), kind=kCustom, calls=%fused_computation.2.clone | custom fusion | bytes 4202496 | tf_op jit(solution)/shard_map/jit(_take)/gather | solution.py:92
  230.5 2.0 fusion.50
  232.5 8.2 %psum.52 = f32[2048]{0:T(1024)S(1)} all-reduce(f32[2048]{0:T(1024)S(1)} %fusion.50), channel_id=1, replica_groups=mesh['dom'=8,'sub'=4] {'sub'}, use_global_device_ids=true, to_apply=%region_16.18 | all-reduce | flops 2048 | bytes 16384 | tf_op jit(solution)/shard_map/psum | solution.py:93
  240.8 39.4 %while.60 = (s32[]{:T(128)}, f32[4096,256]{1,0:T(8,128)}, s32[4,512]{1,0:T(4,128)S(1)}, bf16[4,512,256]{2,1,0:T(8,128)(2,1)S(1)}, f32[4,512]{1,0:T(4,128)S(1)}, /*index=5*/s32[]{:T(128)}, s32[]{:T(128)}) while((s32[]{:T(128)}, f32[4096,256]{1,0:T(8,128)}, s32[4,512]{1,0:T(4,128)S(1)}, bf16[4,512,256]{2,1,0:T(8,128)(2,1)S(1)}, ...), condition=%wide.region_18.20_spmd.clone, body=%wide.region_17.19_spmd.clone.sunk | while | flops 6446907392 | bytes 8663139 | solution.py:96
  240.8 8.6 %fusion.75 = f32[4096,256]{1,0:T(8,128)} fusion(f32[4096,256]{1,0:T(8,128)} %get-tuple-element.574, s32[512]{0:T(512)S(1)} %bitcast.118, pred[]{:T(512)S(6)} %compare.20, f32[512]{0:T(512)S(1)} %bitcast.122, bf16[4,512,256]{2,1,0:T(8,128)(2,1)S(1)} %get-tuple-element.583, s32[]{:T(128)} %get-tuple-element.573), kind=kOutput, calls=%fused_computation.48.clone.1 | convolution fusion | flops 6446907392 | bytes 8654853 | tf_op jit(solution)/shard_map/while/body/eval_jaxpr/dot_general | solution.py:78
  249.5 10.2 %fusion.75 = f32[4096,256]{1,0:T(8,128)} fusion(f32[4096,256]{1,0:T(8,128)} %get-tuple-element.574, s32[512]{0:T(512)S(1)} %bitcast.118, pred[]{:T(512)S(6)} %compare.20, f32[512]{0:T(512)S(1)} %bitcast.122, bf16[4,512,256]{2,1,0:T(8,128)(2,1)S(1)} %get-tuple-element.583, s32[]{:T(128)} %get-tuple-element.573), kind=kOutput, calls=%fused_computation.48.clone.1 | convolution fusion | flops 6446907392 | bytes 8654853 | tf_op jit(solution)/shard_map/while/body/eval_jaxpr/dot_general | solution.py:78
  259.7 10.2 %fusion.75 = f32[4096,256]{1,0:T(8,128)} fusion(f32[4096,256]{1,0:T(8,128)} %get-tuple-element.574, s32[512]{0:T(512)S(1)} %bitcast.118, pred[]{:T(512)S(6)} %compare.20, f32[512]{0:T(512)S(1)} %bitcast.122, bf16[4,512,256]{2,1,0:T(8,128)(2,1)S(1)} %get-tuple-element.583, s32[]{:T(128)} %get-tuple-element.573), kind=kOutput, calls=%fused_computation.48.clone.1 | convolution fusion | flops 6446907392 | bytes 8654853 | tf_op jit(solution)/shard_map/while/body/eval_jaxpr/dot_general | solution.py:78
  269.9 10.2 %fusion.75 = f32[4096,256]{1,0:T(8,128)} fusion(f32[4096,256]{1,0:T(8,128)} %get-tuple-element.574, s32[512]{0:T(512)S(1)} %bitcast.118, pred[]{:T(512)S(6)} %compare.20, f32[512]{0:T(512)S(1)} %bitcast.122, bf16[4,512,256]{2,1,0:T(8,128)(2,1)S(1)} %get-tuple-element.583, s32[]{:T(128)} %get-tuple-element.573), kind=kOutput, calls=%fused_computation.48.clone.1 | convolution fusion | flops 6446907392 | bytes 8654853 | tf_op jit(solution)/shard_map/while/body/eval_jaxpr/dot_general | solution.py:78
  280.1 8.6 %divide_subtract_fusion.1 = f32[4096,256]{1,0:T(8,128)} fusion(f32[4096,256]{1,0:T(8,128)} %divide_subtract_fusion.2, f32[4096,256]{1,0:T(8,128)} %get-tuple-element.167, f32[4096,256]{1,0:T(8,128)} %get-tuple-element.169, f32[4096]{0:T(1024)S(1)} %get-tuple-element.344, f32[4096]{0:T(1024)S(1)} %get-tuple-element.345, f32[4096]{0:T(1024)S(1)} %get-tuple-element.343), kind=kLoop, calls=%fused_computation.73 | loop fusion | flops 6291456 | bytes 16826368 | tf_op jit(solution)/shard_map/sub | solution.py:102
  288.7 10.8 %gather_fusion.6 = f32[2048,256]{1,0:T(8,128)} fusion(f32[4096,256]{1,0:T(8,128)} %divide_subtract_fusion.1, s32[2048]{0:T(1024)S(1)} %fusion.58), kind=kCustom, calls=%fused_computation.3.clone | custom fusion | bytes 4202496 | tf_op jit(solution)/shard_map/jit(_take)/gather | solution.py:92
  299.4 2.0 fusion.51
  301.4 7.0 %psum.53 = f32[2048]{0:T(1024)S(1)} all-reduce(f32[2048]{0:T(1024)S(1)} %fusion.51), channel_id=1, replica_groups=mesh['dom'=8,'sub'=4] {'sub'}, use_global_device_ids=true, to_apply=%region_20.22 | all-reduce | flops 2048 | bytes 16384 | tf_op jit(solution)/shard_map/psum | solution.py:93
  308.5 39.2 %while.61 = (s32[]{:T(128)}, f32[4096,256]{1,0:T(8,128)}, s32[4,512]{1,0:T(4,128)S(1)}, bf16[4,512,256]{2,1,0:T(8,128)(2,1)S(1)}, f32[4,512]{1,0:T(4,128)S(1)}, /*index=5*/s32[]{:T(128)}, s32[]{:T(128)}) while((s32[]{:T(128)}, f32[4096,256]{1,0:T(8,128)}, s32[4,512]{1,0:T(4,128)S(1)}, bf16[4,512,256]{2,1,0:T(8,128)(2,1)S(1)}, ...), condition=%wide.region_22.24_spmd.clone, body=%wide.region_21.23_spmd.clone.sunk | while | flops 6446907392 | bytes 8663139 | solution.py:96
  308.5 8.6 %fusion.76 = f32[4096,256]{1,0:T(8,128)} fusion(f32[4096,256]{1,0:T(8,128)} %get-tuple-element.595, s32[512]{0:T(512)S(1)} %bitcast.119, pred[]{:T(512)S(6)} %compare.21, f32[512]{0:T(512)S(1)} %bitcast.123, bf16[4,512,256]{2,1,0:T(8,128)(2,1)S(1)} %get-tuple-element.604, s32[]{:T(128)} %get-tuple-element.594), kind=kOutput, calls=%fused_computation.59.clone.1 | convolution fusion | flops 6446907392 | bytes 8654853 | tf_op jit(solution)/shard_map/while/body/eval_jaxpr/dot_general | solution.py:78
  317.1 10.2 %fusion.76 = f32[4096,256]{1,0:T(8,128)} fusion(f32[4096,256]{1,0:T(8,128)} %get-tuple-element.595, s32[512]{0:T(512)S(1)} %bitcast.119, pred[]{:T(512)S(6)} %compare.21, f32[512]{0:T(512)S(1)} %bitcast.123, bf16[4,512,256]{2,1,0:T(8,128)(2,1)S(1)} %get-tuple-element.604, s32[]{:T(128)} %get-tuple-element.594), kind=kOutput, calls=%fused_computation.59.clone.1 | convolution fusion | flops 6446907392 | bytes 8654853 | tf_op jit(solution)/shard_map/while/body/eval_jaxpr/dot_general | solution.py:78
  327.3 10.2 %fusion.76 = f32[4096,256]{1,0:T(8,128)} fusion(f32[4096,256]{1,0:T(8,128)} %get-tuple-element.595, s32[512]{0:T(512)S(1)} %bitcast.119, pred[]{:T(512)S(6)} %compare.21, f32[512]{0:T(512)S(1)} %bitcast.123, bf16[4,512,256]{2,1,0:T(8,128)(2,1)S(1)} %get-tuple-element.604, s32[]{:T(128)} %get-tuple-element.594), kind=kOutput, calls=%fused_computation.59.clone.1 | convolution fusion | flops 6446907392 | bytes 8654853 | tf_op jit(solution)/shard_map/while/body/eval_jaxpr/dot_general | solution.py:78
  337.5 10.1 %fusion.76 = f32[4096,256]{1,0:T(8,128)} fusion(f32[4096,256]{1,0:T(8,128)} %get-tuple-element.595, s32[512]{0:T(512)S(1)} %bitcast.119, pred[]{:T(512)S(6)} %compare.21, f32[512]{0:T(512)S(1)} %bitcast.123, bf16[4,512,256]{2,1,0:T(8,128)(2,1)S(1)} %get-tuple-element.604, s32[]{:T(128)} %get-tuple-element.594), kind=kOutput, calls=%fused_computation.59.clone.1 | convolution fusion | flops 6446907392 | bytes 8654853 | tf_op jit(solution)/shard_map/while/body/eval_jaxpr/dot_general | solution.py:78
  347.6 8.5 %divide_subtract_fusion = f32[4096,256]{1,0:T(8,128)} fusion(f32[4096,256]{1,0:T(8,128)} %divide_subtract_fusion.1, f32[4096,256]{1,0:T(8,128)} %get-tuple-element.167, f32[4096,256]{1,0:T(8,128)} %get-tuple-element.170, f32[4096]{0:T(1024)S(1)} %get-tuple-element.344, f32[4096]{0:T(1024)S(1)} %get-tuple-element.345, f32[4096]{0:T(1024)S(1)} %get-tuple-element.343), kind=kLoop, calls=%fused_computation.72 | loop fusion | flops 6291456 | bytes 16826368 | tf_op jit(solution)/shard_map/sub | solution.py:102
  356.1 10.7 %gather_fusion.7 = f32[2048,256]{1,0:T(8,128)} fusion(f32[4096,256]{1,0:T(8,128)} %divide_subtract_fusion, s32[2048]{0:T(1024)S(1)} %fusion.58), kind=kCustom, calls=%fused_computation.4.clone | custom fusion | bytes 4202496 | tf_op jit(solution)/shard_map/jit(_take)/gather | solution.py:110
  366.9 2.8 fusion.53
  369.7 13.6 %all-to-all-start.2 = ((bf16[32,64,256]{2,1,0:T(8,128)(2,1)}), bf16[32,64,256]{2,1,0:T(8,128)(2,1)S(1)}, u32[]{:S(2)}, u32[]{:S(2)}) async-start(bf16[32,64,256]{2,1,0:T(8,128)(2,1)} %bitcast.7), calls=%async_computation.2 | async-start | bytes 2097152 | tf_op jit(solution)/shard_map/all_to_all | solution.py:114
  384.6 43.9 %psum.55 = f32[4096]{0:T(1024)S(1)} all-reduce(f32[4096]{0:T(1024)S(1)} %reshape.297), channel_id=1, replica_groups=mesh['dom'=8,'sub'=4] {'dom','sub'}, use_global_device_ids=true, to_apply=%region_26.28 | all-reduce | flops 4096 | bytes 32768 | tf_op jit(solution)/shard_map/psum | solution.py:127
  428.7 0.8 copy.34
  429.8 1.2 gather_fusion.2
  431.3 0.9 fusion.46
  432.2 0.9 reshape.296
  433.1 0.9 broadcast_select_fusion
  434.0 119.1 %all-reduce.3.cloned.1.call-done = f32[4096,4]{0,1:T(4,128)} async-done(((f32[4096,4]{0,1:T(4,128)}), f32[4096,4]{0,1:T(4,128)}) %all-reduce.3.cloned.1.call-update) | async-done | bytes 65552 | tf_op jit(solution)/shard_map/psum | solution.py:127
  553.2 0.7 add_divide_fusion
  (112 shorter events, 6.8 us)
Async XLA Ops:
  7.2 12.9 %copy-start = (bf16[256,1024]{1,0:T(8,128)(2,1)S(1)}, bf16[256,1024]{1,0:T(8,128)(2,1)}, u32[]{:S(2)}) copy-start(bf16[256,1024]{1,0:T(8,128)(2,1)} %param.19) | copy-start | bytes 1572868
  12.8 13.7 %all-to-all-start = ((s32[32,1,64]{2,1,0:T(1,128)}), s32[32,1,64]{2,1,0:T(1,128)S(1)}, u32[]{:S(2)}, u32[]{:S(2)}) async-start(s32[32,1,64]{2,1,0:T(1,128)} %bitcast.2), calls=%async_computation | async-start | bytes 32768 | tf_op jit(solution)/shard_map/all_to_all | solution.py:40
  26.5 29.5 %all-to-all-start.1 = ((bf16[32,64,256]{2,1,0:T(8,128)(2,1)}), bf16[32,64,256]{2,1,0:T(8,128)(2,1)S(1)}, u32[]{:S(2)}, u32[]{:S(2)}) async-start(bf16[32,64,256]{2,1,0:T(8,128)(2,1)} %bitcast.4), calls=%async_computation.1 | async-start | bytes 2097152 | tf_op jit(solution)/shard_map/all_to_all | solution.py:39
  110.8 32.9 %copy-start.5 = (f32[4096]{0:T(1024)S(1)}, f32[4096]{0:T(1024)}, u32[]{:S(2)}) copy-start(f32[4096]{0:T(1024)} %param.23) | copy-start | bytes 49156
  366.9 16.5 %copy-start.3 = (s32[256,256]{1,0:T(8,128)S(1)}, s32[256,256]{1,0:T(8,128)}, u32[]{:S(2)}) copy-start(s32[256,256]{1,0:T(8,128)} %param.21) | copy-start | bytes 786436
  366.9 17.3 %copy-start.6 = (f32[64,16]{0,1:T(8,128)S(1)}, f32[64,16]{0,1:T(8,128)}, u32[]{:S(2)}) copy-start(f32[64,16]{0,1:T(8,128)} %param.25) | copy-start | bytes 12292
  366.9 17.5 %copy-start.4 = (f32[64,16,4]{0,2,1:T(4,128)S(1)}, f32[64,16,4]{0,2,1:T(4,128)}, u32[]{:S(2)}) copy-start(f32[64,16,4]{0,2,1:T(4,128)} %param.24) | copy-start | bytes 49156
  366.9 61.8 %copy-start.2 = (s32[256]{0:T(256)S(1)}, s32[256]{0:T(256)}, u32[]{:S(2)}) copy-start(s32[256]{0:T(256)} %param.20) | copy-start | bytes 3076
  369.7 59.0 %all-to-all-start.2 = ((bf16[32,64,256]{2,1,0:T(8,128)(2,1)}), bf16[32,64,256]{2,1,0:T(8,128)(2,1)S(1)}, u32[]{:S(2)}, u32[]{:S(2)}) async-start(bf16[32,64,256]{2,1,0:T(8,128)(2,1)} %bitcast.7), calls=%async_computation.2 | async-start | bytes 2097152 | tf_op jit(solution)/shard_map/all_to_all | solution.py:114
  383.3 169.9 %all-reduce.3.cloned.1.call-start = ((), (), s32[]{:S(2)}) async-start(), calls=%async_computation.3 | async-start | bytes 131072 | tf_op jit(solution)/shard_map/psum | solution.py:127
  430.9 123.8 %copy-start.1 = (bf16[256,1024]{1,0:T(8,128)(2,1)S(1)}, bf16[256,1024]{1,0:T(8,128)(2,1)}, u32[]{:S(2)}) copy-start(bf16[256,1024]{1,0:T(8,128)(2,1)} %param.19) | copy-start | bytes 1572868
Sparse Core Ops, SparseCore 0:
  433.2 119.8 all-reduce.2
where the time goes:
time: 566 us; the launch traced here: 562 us
  matrix products  182 us (32%)
  waiting for transfers between devices  136 us (24%)
  blocking collectives  79.3 us (14%)
  local copies, waits for them, and re-layouts  66.3 us (12%)
  other arithmetic  59.1 us (10%)
  starting transfers between devices  23.7 us (4%)
  between operations  14.7 us (3%)
    dot_general x16, matrix products, project_step(): lax.dot_general(table, scaled, contract_rows, precision=lax.Precision.HIG...  156 us
    psum x1, waiting for transfers between devices, per_device(): all_sums, all_counts = lax.psum((book_sums, book_counts), ('dom', 'sub'))  119 us
    gather x5, local copies, waits for them, and re-layouts, per_device(): picked = jnp.take(current, safe_ids, axis=0)  53.8 us
    psum x1, blocking collectives, per_device(): all_sums, all_counts = lax.psum((book_sums, book_counts), ('dom', 'sub'))  43.9 us
    psum x4, blocking collectives, per_device(): inner_full = lax.psum(jnp.sum(as_float * picked, axis=1), 'sub')  35.4 us
    sub x4, other arithmetic, per_device(): current - (weight_fractions * filled[:, None] * current + (1.0 - weight_f...  34.2 us
    dot_general x4, matrix products, tally_step(): lax.dot_general(table, rows_b, contract_rows, preferred_element_type=jnp....  24.7 us
    all_to_all x1, waiting for transfers between devices, per_device(): lax.all_to_all(split_rows, ('dom', 'sub'), split_axis=0, concat_axis=0, t...  14.1 us
  transfers between devices with their start and end apart: 4, of which 3 were waited for; matrix products, arithmetic and copies ran while one was open for 3% of the time, Pallas kernels for 0%

commit v1 on v0

--- a/solution.py
+++ b/solution.py
@@ -124,7 +124,7 @@
     ).reshape(m_all * K, DS)
     book_counts = jnp.sum(code_member, axis=0, dtype=jnp.float32).reshape(m_all * K)
     local_sub = codebook.shape[0]
-    all_sums, all_counts = lax.psum((book_sums, book_counts), ("dom", "sub"))
+    all_sums, all_counts = lax.psum(lax.psum((book_sums, book_counts), "sub"), "dom")
     offset = lax.axis_index("sub") * (local_sub * K)
     totals = lax.dynamic_slice_in_dim(all_sums, offset, local_sub * K, 0)
     tallies = lax.dynamic_slice_in_dim(all_counts, offset, local_sub * K, 0)

time: 566 us -> 526 us (0.929)
  waiting for transfers between devices: 136 us -> 109 us
  blocking collectives: 79.3 us -> 63.7 us
    psum x1 -> x2, waiting for transfers between devices: 119 us -> 89.3 us  [the longest x1 55.8 us: per_device(): lax.psum(lax.psum((book_sums, book_counts), 'sub'), 'dom')]
    psum x1, blocking collectives: 43.9 us -> 22.8 us  [per_device(): lax.psum(lax.psum((book_sums, book_counts), 'sub'), 'dom')]
  transfers between devices with their start and end apart: 4 -> 5, of which waited for: 3 -> 5; matrix products, arithmetic and copies ran while one was open for 3% -> 3% of each run, Pallas kernels for 0% -> 0%
where the time goes in v1:
time: 526 us; the launch traced here: 520 us
  matrix products  182 us (35%)
  waiting for transfers between devices  109 us (21%)
  local copies, waits for them, and re-layouts  66.3 us (13%)
  blocking collectives  63.7 us (12%)
  other arithmetic  59.1 us (11%)
  starting transfers between devices  25.5 us (5%)
  between operations  14.6 us (3%)
    dot_general x16, matrix products, project_step(): lax.dot_general(table, scaled, contract_rows, precision=lax.Precision.HIG...  156 us
    psum x1, waiting for transfers between devices, per_device(): lax.psum(lax.psum((book_sums, book_counts), 'sub'), 'dom')  55.8 us
    gather x5, local copies, waits for them, and re-layouts, per_device(): picked = jnp.take(current, safe_ids, axis=0)  53.8 us
    psum x4, blocking collectives, per_device(): inner_full = lax.psum(jnp.sum(as_float * picked, axis=1), 'sub')  40.9 us
    sub x4, other arithmetic, per_device(): current - (weight_fractions * filled[:, None] * current + (1.0 - weight_f...  34.2 us
    psum x1, waiting for transfers between devices, per_device(): lax.psum((book_sums, book_counts), 'sub')  33.5 us
    dot_general x4, matrix products, tally_step(): lax.dot_general(table, rows_b, contract_rows, preferred_element_type=jnp....  24.7 us
    psum x1, blocking collectives, per_device(): lax.psum(lax.psum((book_sums, book_counts), 'sub'), 'dom')  22.8 us
  transfers between devices with their start and end apart: 5, of which 5 were waited for; matrix products, arithmetic and copies ran while one was open for 3% of the time, Pallas kernels for 0%

profile of v1, /device:TPU:1, one launch (start us, length us, event | category | flops | bytes accessed | tf_op | source)
XLA Modules:
  0.0 520.1 jit_solution(15418528127494719410)
XLA Ops:
  8.4 3.6 gather_fusion
  12.8 7.1 %all-to-all-start = ((s32[32,1,64]{2,1,0:T(1,128)}), s32[32,1,64]{2,1,0:T(1,128)S(1)}, u32[]{:S(2)}, u32[]{:S(2)}) async-start(s32[32,1,64]{2,1,0:T(1,128)} %bitcast.2), calls=%async_computation | async-start | bytes 32768 | tf_op jit(solution)/shard_map/all_to_all | solution.py:40
  20.1 2.1 gather_fusion.1
  22.4 1.0 pad_maximum_fusion
  23.5 3.0 all-to-all-done
  26.5 3.0 all-to-all-start.1
  32.0 10.8 %gather_fusion.3 = f32[2048,256]{1,0:T(8,128)} fusion(f32[4096,256]{1,0:T(8,128)} %param.22, s32[2048]{0:T(1024)S(1)} %fusion.58), kind=kCustom, calls=%fused_computation.clone | custom fusion | bytes 4202496 | tf_op jit(solution)/shard_map/jit(_take)/gather | solution.py:92
  42.8 13.2 %all-to-all-done.1 = bf16[32,64,256]{2,1,0:T(8,128)(2,1)S(1)} async-done(((bf16[32,64,256]{2,1,0:T(8,128)(2,1)}), bf16[32,64,256]{2,1,0:T(8,128)(2,1)S(1)}, u32[]{:S(2)}, u32[]{:S(2)}) %all-to-all-start.1) | async-done | bytes 1048608 | tf_op jit(solution)/shard_map/all_to_all | solution.py:39
  56.4 2.0 fusion.48
  58.4 13.2 %all-reduce.1 = (f32[2048]{0:T(1024)S(1)}, f32[2048]{0:T(1024)S(1)}) all-reduce(f32[2048]{0:T(1024)S(1)} %fusion.48, f32[2048]{0:T(1024)S(1)} %reduce_sum.86), channel_id=1, replica_groups=mesh['dom'=8,'sub'=4] {'sub'}, use_global_device_ids=true, to_apply=%region_6.8 | all-reduce | flops 4096 | bytes 32768 | tf_op jit(solution)/shard_map/psum | solution.py:93
  71.7 39.2 %while.58 = (s32[]{:T(128)}, f32[4096,256]{1,0:T(8,128)}, s32[4,512]{1,0:T(4,128)S(1)}, bf16[4,512,256]{2,1,0:T(8,128)(2,1)S(1)}, f32[4,512]{1,0:T(4,128)S(1)}, /*index=5*/s32[]{:T(128)}, s32[]{:T(128)}) while((s32[]{:T(128)}, f32[4096,256]{1,0:T(8,128)}, s32[4,512]{1,0:T(4,128)S(1)}, bf16[4,512,256]{2,1,0:T(8,128)(2,1)S(1)}, ...), condition=%wide.region_10.12_spmd.clone, body=%wide.region_9.11_spmd.clone.sunk | while | flops 6446907392 | bytes 8663139 | solution.py:96
  71.7 8.6 %fusion.73 = f32[4096,256]{1,0:T(8,128)} fusion(f32[4096,256]{1,0:T(8,128)} %get-tuple-element.534, s32[512]{0:T(512)S(1)} %bitcast.114, pred[]{:T(512)S(6)} %compare.18, f32[512]{0:T(512)S(1)} %bitcast.120, bf16[4,512,256]{2,1,0:T(8,128)(2,1)S(1)} %get-tuple-element.543, s32[]{:T(128)} %get-tuple-element.533), kind=kOutput, calls=%fused_computation.26.clone.1 | convolution fusion | flops 6446907392 | bytes 8654853 | tf_op jit(solution)/shard_map/while/body/eval_jaxpr/dot_general | solution.py:78
  80.3 10.2 %fusion.73 = f32[4096,256]{1,0:T(8,128)} fusion(f32[4096,256]{1,0:T(8,128)} %get-tuple-element.534, s32[512]{0:T(512)S(1)} %bitcast.114, pred[]{:T(512)S(6)} %compare.18, f32[512]{0:T(512)S(1)} %bitcast.120, bf16[4,512,256]{2,1,0:T(8,128)(2,1)S(1)} %get-tuple-element.543, s32[]{:T(128)} %get-tuple-element.533), kind=kOutput, calls=%fused_computation.26.clone.1 | convolution fusion | flops 6446907392 | bytes 8654853 | tf_op jit(solution)/shard_map/while/body/eval_jaxpr/dot_general | solution.py:78
  90.5 10.2 %fusion.73 = f32[4096,256]{1,0:T(8,128)} fusion(f32[4096,256]{1,0:T(8,128)} %get-tuple-element.534, s32[512]{0:T(512)S(1)} %bitcast.114, pred[]{:T(512)S(6)} %compare.18, f32[512]{0:T(512)S(1)} %bitcast.120, bf16[4,512,256]{2,1,0:T(8,128)(2,1)S(1)} %get-tuple-element.543, s32[]{:T(128)} %get-tuple-element.533), kind=kOutput, calls=%fused_computation.26.clone.1 | convolution fusion | flops 6446907392 | bytes 8654853 | tf_op jit(solution)/shard_map/while/body/eval_jaxpr/dot_general | solution.py:78
  100.7 10.2 %fusion.73 = f32[4096,256]{1,0:T(8,128)} fusion(f32[4096,256]{1,0:T(8,128)} %get-tuple-element.534, s32[512]{0:T(512)S(1)} %bitcast.114, pred[]{:T(512)S(6)} %compare.18, f32[512]{0:T(512)S(1)} %bitcast.120, bf16[4,512,256]{2,1,0:T(8,128)(2,1)S(1)} %get-tuple-element.543, s32[]{:T(128)} %get-tuple-element.533), kind=kOutput, calls=%fused_computation.26.clone.1 | convolution fusion | flops 6446907392 | bytes 8654853 | tf_op jit(solution)/shard_map/while/body/eval_jaxpr/dot_general | solution.py:78
  110.8 32.9 %while.57 = (s32[]{:T(128)}, f32[4096]{0:T(1024)S(1)}, f32[4096,256]{1,0:T(8,128)}, s32[4,512]{1,0:T(4,128)S(1)}, bf16[4,512,256]{2,1,0:T(8,128)(2,1)S(1)}, /*index=5*/s32[]{:T(128)}, s32[]{:T(128)}) while((s32[]{:T(128)}, f32[4096]{0:T(1024)S(1)}, f32[4096,256]{1,0:T(8,128)}, s32[4,512]{1,0:T(4,128)S(1)}, ...), condition=%wide.region_4.5_spmd.clone, body=%wide.region_2.4_spmd.clone.sunk | while | flops 1086328832 | bytes 8724576 | solution.py:72
  110.8 4.5 fusion.72
  115.4 2.0 convert_reduce_fusion.4
  117.4 6.7 %fusion.72 = f32[4096,256]{1,0:T(8,128)} fusion(f32[4096,256]{1,0:T(8,128)} %get-tuple-element.514, s32[512]{0:T(512)S(1)} %bitcast.115, pred[]{:T(512)S(6)} %compare.17, bf16[4,512,256]{2,1,0:T(8,128)(2,1)S(1)} %get-tuple-element.523, s32[]{:T(128)} %get-tuple-element.512), kind=kOutput, calls=%fused_computation.17.clone.1 | convolution fusion | flops 1077936128 | bytes 8652805 | tf_op jit(solution)/shard_map/while/body/eval_jaxpr/dot_general | solution.py:63
  124.2 2.0 convert_reduce_fusion.4
  126.2 6.7 %fusion.72 = f32[4096,256]{1,0:T(8,128)} fusion(f32[4096,256]{1,0:T(8,128)} %get-tuple-element.514, s32[512]{0:T(512)S(1)} %bitcast.115, pred[]{:T(512)S(6)} %compare.17, bf16[4,512,256]{2,1,0:T(8,128)(2,1)S(1)} %get-tuple-element.523, s32[]{:T(128)} %get-tuple-element.512), kind=kOutput, calls=%fused_computation.17.clone.1 | convolution fusion | flops 1077936128 | bytes 8652805 | tf_op jit(solution)/shard_map/while/body/eval_jaxpr/dot_general | solution.py:63
  132.9 2.0 convert_reduce_fusion.4
  135.0 6.7 %fusion.72 = f32[4096,256]{1,0:T(8,128)} fusion(f32[4096,256]{1,0:T(8,128)} %get-tuple-element.514, s32[512]{0:T(512)S(1)} %bitcast.115, pred[]{:T(512)S(6)} %compare.17, bf16[4,512,256]{2,1,0:T(8,128)(2,1)S(1)} %get-tuple-element.523, s32[]{:T(128)} %get-tuple-element.512), kind=kOutput, calls=%fused_computation.17.clone.1 | convolution fusion | flops 1077936128 | bytes 8652805 | tf_op jit(solution)/shard_map/while/body/eval_jaxpr/dot_general | solution.py:63
  141.7 2.0 convert_reduce_fusion.4
  143.7 8.6 %divide_subtract_fusion.3 = f32[4096,256]{1,0:T(8,128)} fusion(f32[4096,256]{1,0:T(8,128)} %param.22, f32[4096,256]{1,0:T(8,128)} %get-tuple-element.167, f32[4096,256]{1,0:T(8,128)} %get-tuple-element.166, f32[4096]{0:T(1024)S(1)} %get-tuple-element.346, f32[4096]{0:T(1024)S(1)} %get-tuple-element.347, f32[4096]{0:T(1024)S(1)} %get-tuple-element.345), kind=kLoop, calls=%fused_computation.75 | loop fusion | flops 6291456 | bytes 16826368 | tf_op jit(solution)/shard_map/sub | solution.py:102
  152.3 10.7 %gather_fusion.4 = f32[2048,256]{1,0:T(8,128)} fusion(f32[4096,256]{1,0:T(8,128)} %divide_subtract_fusion.3, s32[2048]{0:T(1024)S(1)} %fusion.58), kind=kCustom, calls=%fused_computation.1.clone | custom fusion | bytes 4202496 | tf_op jit(solution)/shard_map/jit(_take)/gather | solution.py:92
  163.1 2.0 fusion.49
  165.1 7.0 %psum.65 = f32[2048]{0:T(1024)S(1)} all-reduce(f32[2048]{0:T(1024)S(1)} %fusion.49), channel_id=1, replica_groups=mesh['dom'=8,'sub'=4] {'sub'}, use_global_device_ids=true, to_apply=%region_12.14 | all-reduce | flops 2048 | bytes 16384 | tf_op jit(solution)/shard_map/psum | solution.py:93
  172.0 39.2 %while.59 = (s32[]{:T(128)}, f32[4096,256]{1,0:T(8,128)}, s32[4,512]{1,0:T(4,128)S(1)}, bf16[4,512,256]{2,1,0:T(8,128)(2,1)S(1)}, f32[4,512]{1,0:T(4,128)S(1)}, /*index=5*/s32[]{:T(128)}, s32[]{:T(128)}) while((s32[]{:T(128)}, f32[4096,256]{1,0:T(8,128)}, s32[4,512]{1,0:T(4,128)S(1)}, bf16[4,512,256]{2,1,0:T(8,128)(2,1)S(1)}, ...), condition=%wide.region_14.16_spmd.clone, body=%wide.region_13.15_spmd.clone.sunk | while | flops 6446907392 | bytes 8663139 | solution.py:96
  172.1 8.6 %fusion.74 = f32[4096,256]{1,0:T(8,128)} fusion(f32[4096,256]{1,0:T(8,128)} %get-tuple-element.555, s32[512]{0:T(512)S(1)} %bitcast.117, pred[]{:T(512)S(6)} %compare.19, f32[512]{0:T(512)S(1)} %bitcast.121, bf16[4,512,256]{2,1,0:T(8,128)(2,1)S(1)} %get-tuple-element.564, s32[]{:T(128)} %get-tuple-element.554), kind=kOutput, calls=%fused_computation.37.clone.1 | convolution fusion | flops 6446907392 | bytes 8654853 | tf_op jit(solution)/shard_map/while/body/eval_jaxpr/dot_general | solution.py:78
  180.7 10.2 %fusion.74 = f32[4096,256]{1,0:T(8,128)} fusion(f32[4096,256]{1,0:T(8,128)} %get-tuple-element.555, s32[512]{0:T(512)S(1)} %bitcast.117, pred[]{:T(512)S(6)} %compare.19, f32[512]{0:T(512)S(1)} %bitcast.121, bf16[4,512,256]{2,1,0:T(8,128)(2,1)S(1)} %get-tuple-element.564, s32[]{:T(128)} %get-tuple-element.554), kind=kOutput, calls=%fused_computation.37.clone.1 | convolution fusion | flops 6446907392 | bytes 8654853 | tf_op jit(solution)/shard_map/while/body/eval_jaxpr/dot_general | solution.py:78
  190.9 10.2 %fusion.74 = f32[4096,256]{1,0:T(8,128)} fusion(f32[4096,256]{1,0:T(8,128)} %get-tuple-element.555, s32[512]{0:T(512)S(1)} %bitcast.117, pred[]{:T(512)S(6)} %compare.19, f32[512]{0:T(512)S(1)} %bitcast.121, bf16[4,512,256]{2,1,0:T(8,128)(2,1)S(1)} %get-tuple-element.564, s32[]{:T(128)} %get-tuple-element.554), kind=kOutput, calls=%fused_computation.37.clone.1 | convolution fusion | flops 6446907392 | bytes 8654853 | tf_op jit(solution)/shard_map/while/body/eval_jaxpr/dot_general | solution.py:78
  201.0 10.2 %fusion.74 = f32[4096,256]{1,0:T(8,128)} fusion(f32[4096,256]{1,0:T(8,128)} %get-tuple-element.555, s32[512]{0:T(512)S(1)} %bitcast.117, pred[]{:T(512)S(6)} %compare.19, f32[512]{0:T(512)S(1)} %bitcast.121, bf16[4,512,256]{2,1,0:T(8,128)(2,1)S(1)} %get-tuple-element.564, s32[]{:T(128)} %get-tuple-element.554), kind=kOutput, calls=%fused_computation.37.clone.1 | convolution fusion | flops 6446907392 | bytes 8654853 | tf_op jit(solution)/shard_map/while/body/eval_jaxpr/dot_general | solution.py:78
  211.2 8.6 %divide_subtract_fusion.2 = f32[4096,256]{1,0:T(8,128)} fusion(f32[4096,256]{1,0:T(8,128)} %divide_subtract_fusion.3, f32[4096,256]{1,0:T(8,128)} %get-tuple-element.167, f32[4096,256]{1,0:T(8,128)} %get-tuple-element.168, f32[4096]{0:T(1024)S(1)} %get-tuple-element.346, f32[4096]{0:T(1024)S(1)} %get-tuple-element.347, f32[4096]{0:T(1024)S(1)} %get-tuple-element.345), kind=kLoop, calls=%fused_computation.74 | loop fusion | flops 6291456 | bytes 16826368 | tf_op jit(solution)/shard_map/sub | solution.py:102
  219.8 10.7 %gather_fusion.5 = f32[2048,256]{1,0:T(8,128)} fusion(f32[4096,256]{1,0:T(8,128)} %divide_subtract_fusion.2, s32[2048]{0:T(1024)S(1)} %fusion.58), kind=kCustom, calls=%fused_computation.2.clone | custom fusion | bytes 4202496 | tf_op jit(solution)/shard_map/jit(_take)/gather | solution.py:92
  230.5 2.0 fusion.50
  232.5 8.2 %psum.66 = f32[2048]{0:T(1024)S(1)} all-reduce(f32[2048]{0:T(1024)S(1)} %fusion.50), channel_id=1, replica_groups=mesh['dom'=8,'sub'=4] {'sub'}, use_global_device_ids=true, to_apply=%region_16.18 | all-reduce | flops 2048 | bytes 16384 | tf_op jit(solution)/shard_map/psum | solution.py:93
  240.8 39.4 %while.60 = (s32[]{:T(128)}, f32[4096,256]{1,0:T(8,128)}, s32[4,512]{1,0:T(4,128)S(1)}, bf16[4,512,256]{2,1,0:T(8,128)(2,1)S(1)}, f32[4,512]{1,0:T(4,128)S(1)}, /*index=5*/s32[]{:T(128)}, s32[]{:T(128)}) while((s32[]{:T(128)}, f32[4096,256]{1,0:T(8,128)}, s32[4,512]{1,0:T(4,128)S(1)}, bf16[4,512,256]{2,1,0:T(8,128)(2,1)S(1)}, ...), condition=%wide.region_18.20_spmd.clone, body=%wide.region_17.19_spmd.clone.sunk | while | flops 6446907392 | bytes 8663139 | solution.py:96
  240.8 8.6 %fusion.75 = f32[4096,256]{1,0:T(8,128)} fusion(f32[4096,256]{1,0:T(8,128)} %get-tuple-element.576, s32[512]{0:T(512)S(1)} %bitcast.118, pred[]{:T(512)S(6)} %compare.20, f32[512]{0:T(512)S(1)} %bitcast.122, bf16[4,512,256]{2,1,0:T(8,128)(2,1)S(1)} %get-tuple-element.585, s32[]{:T(128)} %get-tuple-element.575), kind=kOutput, calls=%fused_computation.48.clone.1 | convolution fusion | flops 6446907392 | bytes 8654853 | tf_op jit(solution)/shard_map/while/body/eval_jaxpr/dot_general | solution.py:78
  249.5 10.2 %fusion.75 = f32[4096,256]{1,0:T(8,128)} fusion(f32[4096,256]{1,0:T(8,128)} %get-tuple-element.576, s32[512]{0:T(512)S(1)} %bitcast.118, pred[]{:T(512)S(6)} %compare.20, f32[512]{0:T(512)S(1)} %bitcast.122, bf16[4,512,256]{2,1,0:T(8,128)(2,1)S(1)} %get-tuple-element.585, s32[]{:T(128)} %get-tuple-element.575), kind=kOutput, calls=%fused_computation.48.clone.1 | convolution fusion | flops 6446907392 | bytes 8654853 | tf_op jit(solution)/shard_map/while/body/eval_jaxpr/dot_general | solution.py:78
  259.7 10.2 %fusion.75 = f32[4096,256]{1,0:T(8,128)} fusion(f32[4096,256]{1,0:T(8,128)} %get-tuple-element.576, s32[512]{0:T(512)S(1)} %bitcast.118, pred[]{:T(512)S(6)} %compare.20, f32[512]{0:T(512)S(1)} %bitcast.122, bf16[4,512,256]{2,1,0:T(8,128)(2,1)S(1)} %get-tuple-element.585, s32[]{:T(128)} %get-tuple-element.575), kind=kOutput, calls=%fused_computation.48.clone.1 | convolution fusion | flops 6446907392 | bytes 8654853 | tf_op jit(solution)/shard_map/while/body/eval_jaxpr/dot_general | solution.py:78
  269.9 10.2 %fusion.75 = f32[4096,256]{1,0:T(8,128)} fusion(f32[4096,256]{1,0:T(8,128)} %get-tuple-element.576, s32[512]{0:T(512)S(1)} %bitcast.118, pred[]{:T(512)S(6)} %compare.20, f32[512]{0:T(512)S(1)} %bitcast.122, bf16[4,512,256]{2,1,0:T(8,128)(2,1)S(1)} %get-tuple-element.585, s32[]{:T(128)} %get-tuple-element.575), kind=kOutput, calls=%fused_computation.48.clone.1 | convolution fusion | flops 6446907392 | bytes 8654853 | tf_op jit(solution)/shard_map/while/body/eval_jaxpr/dot_general | solution.py:78
  280.1 8.6 %divide_subtract_fusion.1 = f32[4096,256]{1,0:T(8,128)} fusion(f32[4096,256]{1,0:T(8,128)} %divide_subtract_fusion.2, f32[4096,256]{1,0:T(8,128)} %get-tuple-element.167, f32[4096,256]{1,0:T(8,128)} %get-tuple-element.169, f32[4096]{0:T(1024)S(1)} %get-tuple-element.346, f32[4096]{0:T(1024)S(1)} %get-tuple-element.347, f32[4096]{0:T(1024)S(1)} %get-tuple-element.345), kind=kLoop, calls=%fused_computation.73 | loop fusion | flops 6291456 | bytes 16826368 | tf_op jit(solution)/shard_map/sub | solution.py:102
  288.7 10.8 %gather_fusion.6 = f32[2048,256]{1,0:T(8,128)} fusion(f32[4096,256]{1,0:T(8,128)} %divide_subtract_fusion.1, s32[2048]{0:T(1024)S(1)} %fusion.58), kind=kCustom, calls=%fused_computation.3.clone | custom fusion | bytes 4202496 | tf_op jit(solution)/shard_map/jit(_take)/gather | solution.py:92
  299.4 2.0 fusion.51
  301.4 12.5 %all-reduce = (f32[2048]{0:T(1024)S(1)}, f32[4096]{0:T(1024)S(1)}) all-reduce(f32[2048]{0:T(1024)S(1)} %fusion.51, f32[4096]{0:T(1024)S(1)} %reshape.297), channel_id=1, replica_groups=mesh['dom'=8,'sub'=4] {'sub'}, use_global_device_ids=true, to_apply=%region_20.22 | all-reduce | flops 6144 | bytes 49152 | tf_op jit(solution)/shard_map/psum | solution.py:93
  314.0 39.2 %while.61 = (s32[]{:T(128)}, f32[4096,256]{1,0:T(8,128)}, s32[4,512]{1,0:T(4,128)S(1)}, bf16[4,512,256]{2,1,0:T(8,128)(2,1)S(1)}, f32[4,512]{1,0:T(4,128)S(1)}, /*index=5*/s32[]{:T(128)}, s32[]{:T(128)}) while((s32[]{:T(128)}, f32[4096,256]{1,0:T(8,128)}, s32[4,512]{1,0:T(4,128)S(1)}, bf16[4,512,256]{2,1,0:T(8,128)(2,1)S(1)}, ...), condition=%wide.region_22.24_spmd.clone, body=%wide.region_21.23_spmd.clone.sunk | while | flops 6446907392 | bytes 8663139 | solution.py:96
  314.0 8.6 %fusion.76 = f32[4096,256]{1,0:T(8,128)} fusion(f32[4096,256]{1,0:T(8,128)} %get-tuple-element.597, s32[512]{0:T(512)S(1)} %bitcast.119, pred[]{:T(512)S(6)} %compare.21, f32[512]{0:T(512)S(1)} %bitcast.123, bf16[4,512,256]{2,1,0:T(8,128)(2,1)S(1)} %get-tuple-element.606, s32[]{:T(128)} %get-tuple-element.596), kind=kOutput, calls=%fused_computation.59.clone.1 | convolution fusion | flops 6446907392 | bytes 8654853 | tf_op jit(solution)/shard_map/while/body/eval_jaxpr/dot_general | solution.py:78
  322.6 10.2 %fusion.76 = f32[4096,256]{1,0:T(8,128)} fusion(f32[4096,256]{1,0:T(8,128)} %get-tuple-element.597, s32[512]{0:T(512)S(1)} %bitcast.119, pred[]{:T(512)S(6)} %compare.21, f32[512]{0:T(512)S(1)} %bitcast.123, bf16[4,512,256]{2,1,0:T(8,128)(2,1)S(1)} %get-tuple-element.606, s32[]{:T(128)} %get-tuple-element.596), kind=kOutput, calls=%fused_computation.59.clone.1 | convolution fusion | flops 6446907392 | bytes 8654853 | tf_op jit(solution)/shard_map/while/body/eval_jaxpr/dot_general | solution.py:78
  332.8 10.2 %fusion.76 = f32[4096,256]{1,0:T(8,128)} fusion(f32[4096,256]{1,0:T(8,128)} %get-tuple-element.597, s32[512]{0:T(512)S(1)} %bitcast.119, pred[]{:T(512)S(6)} %compare.21, f32[512]{0:T(512)S(1)} %bitcast.123, bf16[4,512,256]{2,1,0:T(8,128)(2,1)S(1)} %get-tuple-element.606, s32[]{:T(128)} %get-tuple-element.596), kind=kOutput, calls=%fused_computation.59.clone.1 | convolution fusion | flops 6446907392 | bytes 8654853 | tf_op jit(solution)/shard_map/while/body/eval_jaxpr/dot_general | solution.py:78
  343.0 10.2 %fusion.76 = f32[4096,256]{1,0:T(8,128)} fusion(f32[4096,256]{1,0:T(8,128)} %get-tuple-element.597, s32[512]{0:T(512)S(1)} %bitcast.119, pred[]{:T(512)S(6)} %compare.21, f32[512]{0:T(512)S(1)} %bitcast.123, bf16[4,512,256]{2,1,0:T(8,128)(2,1)S(1)} %get-tuple-element.606, s32[]{:T(128)} %get-tuple-element.596), kind=kOutput, calls=%fused_computation.59.clone.1 | convolution fusion | flops 6446907392 | bytes 8654853 | tf_op jit(solution)/shard_map/while/body/eval_jaxpr/dot_general | solution.py:78
  353.1 8.5 %divide_subtract_fusion = f32[4096,256]{1,0:T(8,128)} fusion(f32[4096,256]{1,0:T(8,128)} %divide_subtract_fusion.1, f32[4096,256]{1,0:T(8,128)} %get-tuple-element.167, f32[4096,256]{1,0:T(8,128)} %get-tuple-element.170, f32[4096]{0:T(1024)S(1)} %get-tuple-element.346, f32[4096]{0:T(1024)S(1)} %get-tuple-element.347, f32[4096]{0:T(1024)S(1)} %get-tuple-element.345), kind=kLoop, calls=%fused_computation.72 | loop fusion | flops 6291456 | bytes 16826368 | tf_op jit(solution)/shard_map/sub | solution.py:102
  361.6 10.7 %gather_fusion.7 = f32[2048,256]{1,0:T(8,128)} fusion(f32[4096,256]{1,0:T(8,128)} %divide_subtract_fusion, s32[2048]{0:T(1024)S(1)} %fusion.58), kind=kCustom, calls=%fused_computation.4.clone | custom fusion | bytes 4202496 | tf_op jit(solution)/shard_map/jit(_take)/gather | solution.py:110
  372.4 2.8 fusion.53
  375.2 15.3 %all-to-all-start.2 = ((bf16[32,64,256]{2,1,0:T(8,128)(2,1)}), bf16[32,64,256]{2,1,0:T(8,128)(2,1)S(1)}, u32[]{:S(2)}, u32[]{:S(2)}) async-start(bf16[32,64,256]{2,1,0:T(8,128)(2,1)} %bitcast.7), calls=%async_computation.2 | async-start | bytes 2097152 | tf_op jit(solution)/shard_map/all_to_all | solution.py:114
  391.0 22.8 %psum.71 = f32[4096]{0:T(1024)S(1)} all-reduce(f32[4096]{0:T(1024)S(1)} %get-tuple-element.336), channel_id=1, replica_groups=mesh['dom'=8,'sub'=4] {'dom'}, use_global_device_ids=true, to_apply=%region_28.30 | all-reduce | flops 4096 | bytes 32768 | tf_op jit(solution)/shard_map/psum | solution.py:127
  413.9 3.0 all-to-all-done.2
  416.8 0.8 copy.34
  417.9 1.2 gather_fusion.2
  419.4 0.9 fusion.46
  420.3 0.9 reshape.296
  421.3 33.5 %all-reduce.5.cloned.1.call-done = f32[4096,4]{0,1:T(4,128)} async-done(((f32[4096,4]{0,1:T(4,128)}), f32[4096,4]{0,1:T(4,128)}) %all-reduce.5.cloned.1.call-update) | async-done | bytes 65552 | tf_op jit(solution)/shard_map/psum | solution.py:127
  454.8 0.9 broadcast_select_fusion
  455.7 55.8 %all-reduce.7.cloned.1.call-done = f32[4096,4]{0,1:T(4,128)} async-done(((f32[4096,4]{0,1:T(4,128)}), f32[4096,4]{0,1:T(4,128)}) %all-reduce.7.cloned.1.call-update) | async-done | bytes 65552 | tf_op jit(solution)/shard_map/psum | solution.py:127
  (115 shorter events, 8.4 us)
Async XLA Ops:
  7.2 12.9 %copy-start = (bf16[256,1024]{1,0:T(8,128)(2,1)S(1)}, bf16[256,1024]{1,0:T(8,128)(2,1)}, u32[]{:S(2)}) copy-start(bf16[256,1024]{1,0:T(8,128)(2,1)} %param.19) | copy-start | bytes 1572868
  12.8 13.7 %all-to-all-start = ((s32[32,1,64]{2,1,0:T(1,128)}), s32[32,1,64]{2,1,0:T(1,128)S(1)}, u32[]{:S(2)}, u32[]{:S(2)}) async-start(s32[32,1,64]{2,1,0:T(1,128)} %bitcast.2), calls=%async_computation | async-start | bytes 32768 | tf_op jit(solution)/shard_map/all_to_all | solution.py:40
  22.1 7.5 %copy-start.3 = (s32[256,256]{1,0:T(8,128)S(1)}, s32[256,256]{1,0:T(8,128)}, u32[]{:S(2)}) copy-start(s32[256,256]{1,0:T(8,128)} %param.21) | copy-start | bytes 786436
  26.5 29.5 %all-to-all-start.1 = ((bf16[32,64,256]{2,1,0:T(8,128)(2,1)}), bf16[32,64,256]{2,1,0:T(8,128)(2,1)S(1)}, u32[]{:S(2)}, u32[]{:S(2)}) async-start(bf16[32,64,256]{2,1,0:T(8,128)(2,1)} %bitcast.4), calls=%async_computation.1 | async-start | bytes 2097152 | tf_op jit(solution)/shard_map/all_to_all | solution.py:39
  110.8 32.9 %copy-start.5 = (f32[4096]{0:T(1024)S(1)}, f32[4096]{0:T(1024)}, u32[]{:S(2)}) copy-start(f32[4096]{0:T(1024)} %param.23) | copy-start | bytes 49156
  372.4 18.1 %copy-start.6 = (f32[64,16]{0,1:T(8,128)S(1)}, f32[64,16]{0,1:T(8,128)}, u32[]{:S(2)}) copy-start(f32[64,16]{0,1:T(8,128)} %param.25) | copy-start | bytes 12292
  372.4 18.3 %copy-start.4 = (f32[64,16,4]{0,2,1:T(4,128)S(1)}, f32[64,16,4]{0,2,1:T(4,128)}, u32[]{:S(2)}) copy-start(f32[64,16,4]{0,2,1:T(4,128)} %param.24) | copy-start | bytes 49156
  372.4 18.6 %copy-start.2 = (s32[256]{0:T(256)S(1)}, s32[256]{0:T(256)}, u32[]{:S(2)}) copy-start(s32[256]{0:T(256)} %param.20) | copy-start | bytes 3076
  375.2 41.6 %all-to-all-start.2 = ((bf16[32,64,256]{2,1,0:T(8,128)(2,1)}), bf16[32,64,256]{2,1,0:T(8,128)(2,1)S(1)}, u32[]{:S(2)}, u32[]{:S(2)}) async-start(bf16[32,64,256]{2,1,0:T(8,128)(2,1)} %bitcast.7), calls=%async_computation.2 | async-start | bytes 2097152 | tf_op jit(solution)/shard_map/all_to_all | solution.py:114
  390.5 64.3 %all-reduce.5.cloned.1.call-start = ((), (), s32[]{:S(2)}) async-start(), calls=%async_computation.3 | async-start | bytes 131072 | tf_op jit(solution)/shard_map/psum | solution.py:127
  419.0 94.1 %copy-start.1 = (bf16[256,1024]{1,0:T(8,128)(2,1)S(1)}, bf16[256,1024]{1,0:T(8,128)(2,1)}, u32[]{:S(2)}) copy-start(bf16[256,1024]{1,0:T(8,128)(2,1)} %param.19) | copy-start | bytes 1572868
  421.2 90.3 %all-reduce.7.cloned.1.call-start = ((), (), s32[]{:S(2)}) async-start(), calls=%async_computation.4 | async-start | bytes 131072 | tf_op jit(solution)/shard_map/psum | solution.py:127
Sparse Core Ops, SparseCore 0:
  421.4 33.3 all-reduce.4
  458.1 53.3 all-reduce.6
